TPU v7x, 256 devices: a whole 4x4x8 slice. The times are simulated.
256 devices in a mesh: section: 16 (over y, x_hi, core), expert: 16 (over x_lo, z).
Axes of the slice: x: 4 (x_hi: 2, x_lo: 2; x = x_hi * 2 + x_lo), y: 4, z: 8, core: 2. Of those that a mesh axis runs over, the one named last changes fastest.
Arguments:
- tokens: bfloat16 [16, 2048, 7168], P('section', 'expert'), may hold values from -6 to 6
- cotangent: bfloat16 [16, 2048, 7168], P('section', 'expert'), may hold values from -6 to 6
- expert_ids: int32 [16, 2048, 8], P('section', 'expert'), may hold values from 0 to 31, as said below
- slot_index: int32 [16, 2048, 8], P('section', 'expert'), may hold values from 0 to 31, as said below
- gate_scale: float32 [16, 2048, 8], P('section', 'expert'), may hold values from 0.2 to 1.2
- gate_weight: bfloat16 [16, 7168, 2048], P('section', None, 'expert'), may hold values from -0.0625 to 0.0625
- up_weight: bfloat16 [16, 7168, 2048], P('section', None, 'expert'), may hold values from -0.0625 to 0.0625
- down_weight: bfloat16 [16, 2048, 7168], P('section', 'expert'), may hold values from -0.125 to 0.125
Outputs:
- next_input: bfloat16 [16, 2048, 7168], P('section', 'expert')
- prior_grad: bfloat16 [16, 2048, 7168], P('section', 'expert')
Inputs may be any that keep to these rules, and one draw needn't show every extreme that they name: `expert_ids`: each token names 8 different experts; among the 128 tokens of one device every expert is named exactly 32 times. `slot_index`: among the routes of one device's tokens to one expert, the slots are 0 to 31, each once.
All inputs are finite; a program needn't handle non-finite values.
Results may differ from a plain program's by a relative error of at most 0.011.
Values may be sent and summed in bfloat16 or wider, within the bound.
No kernel may reach another device: no remote copies, remote signals or barrier semaphores. Data moves between devices by JAX's collectives and lax.ppermute only.
A program may use at most 128 MiB of HBM per device.

v0:
```python
import jax
import jax.numpy as jnp
from jax import lax
from jax.sharding import PartitionSpec as P

CAP = 32


def from_behind(x, axis, by):
    length = lax.axis_size(axis)
    pairs = [(i, i + by) for i in range(length) if 0 <= i + by < length]
    return lax.ppermute(x, axis, pairs)


def silu_parts(gate):
    sig = jax.nn.sigmoid(gate)
    return (gate * sig, sig * (1.0 + gate * (1.0 - sig)))


def body(
    tokens, cotangent, expert_ids, slot_index, gate_scale, gate_weight, up_weight, down_weight
):
    section = lax.axis_index("section")
    local = tokens[0]
    grad_out = cotangent[0]
    named = expert_ids[0]
    gate_mat = gate_weight[0]
    up_mat = up_weight[0]
    down_mat = down_weight[0]
    width_local = gate_mat.shape[1]
    hit = named == section
    chosen = jnp.any(hit, axis=1)
    slot = jnp.sum(jnp.where(hit, slot_index[0], 0), axis=1)
    weight = jnp.sum(jnp.where(hit, gate_scale[0], jnp.float32(0.0)), axis=1)
    places = jnp.arange(CAP, dtype=jnp.int32)
    table = ((places[:, None] == slot[None, :]) & chosen[None, :]).astype(jnp.bfloat16)
    sent = jnp.dot(table, local, preferred_element_type=jnp.float32).astype(jnp.bfloat16)
    carried = (weight[:, None] * grad_out.astype(jnp.float32)).astype(jnp.bfloat16)
    back = jnp.dot(table, carried, preferred_element_type=jnp.float32).astype(jnp.bfloat16)
    piece = lax.all_gather(sent, "expert", axis=0, tiled=True)
    gate_up = jnp.concatenate(
        [
            jnp.dot(piece, gate_mat, preferred_element_type=jnp.float32),
            jnp.dot(piece, up_mat, preferred_element_type=jnp.float32),
        ],
        axis=1,
    )
    gate = gate_up[:, :width_local]
    up = gate_up[:, width_local:]
    act, slope = silu_parts(gate)
    hidden = (act * up).astype(jnp.bfloat16)
    combined = lax.psum_scatter(
        jnp.dot(hidden, down_mat, preferred_element_type=jnp.float32).astype(jnp.bfloat16),
        "expert",
        scatter_dimension=0,
        tiled=True,
    ).astype(jnp.float32)
    grad_hidden = jnp.dot(
        lax.all_gather(back, "expert", axis=0, tiled=True),
        down_mat.T,
        preferred_element_type=jnp.float32,
    )
    grad_up = (grad_hidden * act).astype(jnp.bfloat16)
    grad_gate = (grad_hidden * up * slope).astype(jnp.bfloat16)
    behind = jnp.dot(grad_gate, gate_mat.T, preferred_element_type=jnp.float32)
    inward = lax.psum_scatter(
        (behind + jnp.dot(grad_up, up_mat.T, preferred_element_type=jnp.float32)).astype(
            jnp.bfloat16
        ),
        "expert",
        scatter_dimension=0,
        tiled=True,
    ).astype(jnp.float32)
    output = local.astype(jnp.float32) + weight[:, None] * jnp.take(combined, slot, axis=0)
    grad_in = grad_out.astype(jnp.float32) + jnp.where(
        chosen[:, None], jnp.take(inward, slot, axis=0), jnp.float32(0.0)
    )
    next_input = from_behind(output.astype(jnp.bfloat16)[None], "section", 1)
    prior_grad = from_behind(grad_in.astype(jnp.bfloat16)[None], "section", -1)
    return (next_input, prior_grad)


def solution(mesh):
    in_specs = (
        P("section", "expert", None),
        P("section", "expert", None),
        P("section", "expert", None),
        P("section", "expert", None),
        P("section", "expert", None),
        P("section", None, "expert"),
        P("section", None, "expert"),
        P("section", "expert", None),
    )
    out_specs = (P("section", "expert", None), P("section", "expert", None))
    return jax.shard_map(body, mesh=mesh, in_specs=in_specs, out_specs=out_specs, check_vma=False)
```

profile of v0, /device:TPU:1, one launch (start us, length us, event | category | flops | bytes accessed | tf_op | source)
XLA Modules:
  0.0 467.2 jit_solution(15120559337887811934)
XLA Ops:
  7.2 0.0 copy-start
  7.2 0.0 all-gather.3.cloned.1.call-start
  7.2 0.8 select_reduce_fusion.1
  8.1 0.7 select_reduce_fusion
  8.8 2.6 convolution_convert_fusion.2
  11.4 0.0 all-gather.3.cloned.1.call-update
  11.5 0.0 all-gather.5.cloned.1.call-start
  11.5 2.8 convolution_convert_fusion.1
  14.3 0.0 all-gather.5.cloned.1.call-update
  14.3 0.0 reduce-scatter.5.cloned.1.call-start
  14.4 91.3 %all-gather.3.cloned.1.call-done = bf16[512,7168]{1,0:T(8,128)(2,1)} async-done(((bf16[32,7168]{1,0:T(8,128)(2,1)}), bf16[512,7168]{1,0:T(8,128)(2,1)}) %all-gather.3.cloned.1.call-update) | async-done | bytes 7340048 | tf_op jit(solution)/shard_map/all_gather | solution.py:40
  105.6 0.0 copy-done
  105.6 0.0 copy-start.2
  105.6 0.0 copy-start.5
  105.6 5.3 %fusion.16 = f32[512,128]{1,0:T(8,128)S(1)} fusion(bf16[512,7168]{1,0:T(8,128)(2,1)} %all-gather.3.cloned.1.call-done, bf16[1,7168,128]{2,1,0:T(8,128)(2,1)S(1)} %copy-done), kind=kOutput, calls=%fused_computation.25 | convolution fusion | flops 939524096 | bytes 9437184 | tf_op jit(solution)/shard_map/dot_general | solution.py:43
  110.9 0.0 copy-done.2
  110.9 0.4 copy-done.5
  111.4 2.1 fusion.12
  113.4 82.7 %all-gather.5.cloned.1.call-done = bf16[512,7168]{1,0:T(8,128)(2,1)} async-done(((bf16[32,7168]{1,0:T(8,128)(2,1)}), bf16[512,7168]{1,0:T(8,128)(2,1)}) %all-gather.5.cloned.1.call-update) | async-done | bytes 7340048 | tf_op jit(solution)/shard_map/all_gather | solution.py:59
  196.1 5.6 %fusion.8 = f32[512,128]{1,0:T(8,128)S(1)} fusion(bf16[512,7168]{1,0:T(8,128)(2,1)} %all-gather.5.cloned.1.call-done, bf16[1,128,7168]{2,1,0:T(8,128)(2,1)} %param.17), kind=kOutput, calls=%fused_computation.17 | convolution fusion | flops 939524096 | bytes 9437184 | tf_op jit(solution)/shard_map/dot_general | solution.py:58
  201.8 0.0 copy-start.3
  201.8 7.3 %fusion.14 = f32[512,7168]{1,0:T(8,128)} fusion(bf16[1,7168,128]{2,1,0:T(8,128)(2,1)S(1)} %copy-done, f32[512,128]{1,0:T(8,128)S(1)} %fusion.16, f32[512,128]{1,0:T(8,128)S(1)} %fusion.8, f32[512,128]{1,0:T(8,128)S(1)} %fusion.12), kind=kOutput, calls=%fused_computation.23 | convolution fusion | flops 940179456 | bytes 17301504 | tf_op jit(solution)/shard_map/dot_general | solution.py:65
  209.1 0.0 copy-done.3
  209.1 10.2 %add_convert_fusion = bf16[512,7168]{1,0:T(8,128)(2,1)} fusion(f32[512,7168]{1,0:T(8,128)} %fusion.14, bf16[1,7168,128]{2,1,0:T(8,128)(2,1)S(1)} %copy-done.3, f32[512,128]{1,0:T(8,128)S(1)} %fusion.8, f32[512,128]{1,0:T(8,128)S(1)} %fusion.16), kind=kOutput, calls=%fused_computation.2 | convolution fusion | flops 947257344 | bytes 24379392 | tf_op jit(solution)/shard_map/dot_general | solution.py:67
  219.3 0.0 copy-start.4
  219.3 0.0 reduce-scatter.5.cloned.1.call-update
  219.3 0.2 reduce-scatter.3.cloned.1.call-start
  219.5 1.2 copy-done.4
  220.8 5.0 %convolution_convert_fusion = bf16[512,7168]{1,0:T(8,128)(2,1)} fusion(bf16[1,128,7168]{2,1,0:T(8,128)(2,1)S(1)} %copy-done.4, f32[512,128]{1,0:T(8,128)S(1)} %fusion.12, f32[512,128]{1,0:T(8,128)S(1)} %fusion.16), kind=kOutput, calls=%fused_computation.3 | convolution fusion | flops 943587328 | bytes 9699328 | tf_op jit(solution)/shard_map/dot_general | solution.py:53
  225.8 0.0 reduce-scatter.3.cloned.1.call-update
  225.9 80.5 %reduce-scatter.5.cloned.1.call-done = bf16[32,7168]{1,0:T(8,128)(2,1)} async-done(((bf16[512,7168]{1,0:T(8,128)(2,1)}), bf16[32,7168]{1,0:T(8,128)(2,1)}) %reduce-scatter.5.cloned.1.call-update) | async-done | bytes 458768 | tf_op jit(solution)/shard_map/reduce_scatter | solution.py:66
  306.3 1.1 convert_element_type.60
  307.4 3.6 gather_fusion.1
  311.0 87.2 %reduce-scatter.3.cloned.1.call-done = bf16[32,7168]{1,0:T(8,128)(2,1)} async-done(((bf16[512,7168]{1,0:T(8,128)(2,1)}), bf16[32,7168]{1,0:T(8,128)(2,1)}) %reduce-scatter.3.cloned.1.call-update) | async-done | bytes 458768 | tf_op jit(solution)/shard_map/reduce_scatter | solution.py:52
  398.2 1.1 convert_element_type.51
  399.2 3.4 gather_fusion
  402.7 5.7 %fusion.5 = (bf16[1,128,7168]{2,1,0:T(8,128)(2,1)S(1)}, bf16[1,128,7168]{2,1,0:T(8,128)(2,1)S(1)}) fusion(f32[128,7168]{1,0:T(8,128)} %gather_fusion.1, bf16[1,128,7168]{2,1,0:T(8,128)(2,1)} %param.11, pred[128]{0:T(512)(128)(4,1)S(1)} %compare_and_fusion, pred[128]{0:T(512)(128)(4,1)S(1)} %reduce_or.9, f32[128,7168]{1,0:T(8,128)} %gather_fusion, ...), kind=kLoop, calls=%fused_computation.15 | loop fusion | flops 9175040 | bytes 14680832 | tf_op jit(solution)/shard_map/broadcast_in_dim | solution.py:79
  408.4 8.2 %collective-permute-start = (bf16[1,128,7168]{2,1,0:T(8,128)(2,1)S(1)}, bf16[1,128,7168]{2,1,0:T(8,128)(2,1)S(1)}, u32[]{:S(2)}, u32[]{:S(2)}) collective-permute-start(bf16[1,128,7168]{2,1,0:T(8,128)(2,1)S(1)} %get-tuple-element.6), channel_id=1, source_target_pairs={{0,16},{16,32},{32,48},{48,64},{64,80},{80,96},{96,112},{112,128},... | collective-permute-start | bytes 5505032 | tf_op jit(solution)/shard_map/ppermute | solution.py:12
  416.6 0.0 copy-start.1
  416.6 2.1 collective-permute-start.1
  418.6 18.1 %collective-permute-done = bf16[1,128,7168]{2,1,0:T(8,128)(2,1)S(1)} collective-permute-done((bf16[1,128,7168]{2,1,0:T(8,128)(2,1)S(1)}, bf16[1,128,7168]{2,1,0:T(8,128)(2,1)S(1)}, u32[]{:S(2)}, u32[]{:S(2)}) %collective-permute-start) | collective-permute-done | bytes 1835040 | tf_op jit(solution)/shard_map/ppermute | solution.py:12
  436.7 21.5 %collective-permute-done.1 = bf16[1,128,7168]{2,1,0:T(8,128)(2,1)S(1)} collective-permute-done((bf16[1,128,7168]{2,1,0:T(8,128)(2,1)S(1)}, bf16[1,128,7168]{2,1,0:T(8,128)(2,1)S(1)}, u32[]{:S(2)}, u32[]{:S(2)}) %collective-permute-start.1) | collective-permute-done | bytes 1835040 | tf_op jit(solution)/shard_map/ppermute | solution.py:12
  458.2 1.2 copy.12
  459.5 1.2 copy.13
  460.7 0.0 copy-done.1
  (4 shorter events, 0.0 us)
Async XLA Ops:
  7.2 98.5 %copy-start = (bf16[1,7168,128]{2,1,0:T(8,128)(2,1)S(1)}, bf16[1,7168,128]{2,1,0:T(8,128)(2,1)}, u32[]{:S(2)}) copy-start(bf16[1,7168,128]{2,1,0:T(8,128)(2,1)} %param.15) | copy-start | bytes 5505028
  7.2 98.5 %all-gather.3.cloned.1.call-start = ((), (), s32[]{:S(2)}) async-start(), calls=%async_computation.2 | async-start | bytes 7798784 | tf_op jit(solution)/shard_map/all_gather | solution.py:40
  11.5 184.7 %all-gather.5.cloned.1.call-start = ((), (), s32[]{:S(2)}) async-start(), calls=%async_computation.4 | async-start | bytes 7798784 | tf_op jit(solution)/shard_map/all_gather | solution.py:59
  14.3 292.0 %reduce-scatter.5.cloned.1.call-start = ((), (), s32[]{:S(2)}) async-start(), calls=%async_computation.5 | async-start | bytes 7798784 | tf_op jit(solution)/shard_map/reduce_scatter | solution.py:66
  105.6 5.3 %copy-start.2 = (bf16[1,7168,128]{2,1,0:T(8,128)(2,1)S(1)}, bf16[1,7168,128]{2,1,0:T(8,128)(2,1)}, u32[]{:S(2)}) copy-start(bf16[1,7168,128]{2,1,0:T(8,128)(2,1)} %param.16) | copy-start | bytes 5505028
  105.6 5.7 %copy-start.5 = (bf16[512,7168]{1,0:T(8,128)(2,1)S(1)}, bf16[512,7168]{1,0:T(8,128)(2,1)}, u32[]{:S(2)}) copy-start(bf16[512,7168]{1,0:T(8,128)(2,1)} %all-gather.3.cloned.1.call-done) | copy-start | bytes 22020100
  201.8 7.3 %copy-start.3 = (bf16[1,7168,128]{2,1,0:T(8,128)(2,1)S(1)}, bf16[1,7168,128]{2,1,0:T(8,128)(2,1)}, u32[]{:S(2)}) copy-start(bf16[1,7168,128]{2,1,0:T(8,128)(2,1)} %param.16) | copy-start | bytes 5505028
  219.3 1.5 copy-start.4
  219.3 178.9 %reduce-scatter.3.cloned.1.call-start = ((), (), s32[]{:S(2)}) async-start(), calls=%async_computation.3 | async-start | bytes 7798784 | tf_op jit(solution)/shard_map/reduce_scatter | solution.py:52
  408.4 28.3 %collective-permute-start = (bf16[1,128,7168]{2,1,0:T(8,128)(2,1)S(1)}, bf16[1,128,7168]{2,1,0:T(8,128)(2,1)S(1)}, u32[]{:S(2)}, u32[]{:S(2)}) collective-permute-start(bf16[1,128,7168]{2,1,0:T(8,128)(2,1)S(1)} %get-tuple-element.6), channel_id=1, source_target_pairs={{0,16},{16,32},{32,48},{48,64},{64,80},{80,96},{96,112},{112,128},... | collective-permute-start | bytes 5505032 | tf_op jit(solution)/shard_map/ppermute | solution.py:12
  416.6 44.1 %copy-start.1 = (bf16[1,7168,128]{2,1,0:T(8,128)(2,1)S(1)}, bf16[1,7168,128]{2,1,0:T(8,128)(2,1)}, u32[]{:S(2)}) copy-start(bf16[1,7168,128]{2,1,0:T(8,128)(2,1)} %param.15) | copy-start | bytes 5505028
  416.6 41.7 %collective-permute-start.1 = (bf16[1,128,7168]{2,1,0:T(8,128)(2,1)S(1)}, bf16[1,128,7168]{2,1,0:T(8,128)(2,1)S(1)}, u32[]{:S(2)}, u32[]{:S(2)}) collective-permute-start(bf16[1,128,7168]{2,1,0:T(8,128)(2,1)S(1)} %get-tuple-element.5), channel_id=1, source_target_pairs={{16,0},{32,16},{48,32},{64,48},{80,64},{96,80},{112,96},{128,112},... | collective-permute-start | bytes 5505032 | tf_op jit(solution)/shard_map/ppermute | solution.py:12
Sparse Core Ops, SparseCore 0:
  11.6 94.0 all-gather.2
  108.0 88.0 all-gather.4
  219.4 86.8 reduce-scatter.4
  308.7 89.3 reduce-scatter.2
where the time goes:
time: 468 us; the launch traced here: 467 us
  waiting for transfers between devices  381 us (81%)
  matrix products  40.9 us (9%)
  between operations  13.9 us (3%)
  local copies, waits for them, and re-layouts  11.2 us (2%)
  starting transfers between devices  10.6 us (2%)
  other arithmetic  9.46 us (2%)
    all_gather x1, waiting for transfers between devices, body(): piece = lax.all_gather(sent, 'expert', axis=0, tiled=True)  91.3 us
    reduce_scatter x1, waiting for transfers between devices, body(): lax.psum_scatter(jnp.dot(hidden, down_mat, preferred_element_type=jnp.flo...  87.2 us
    all_gather x1, waiting for transfers between devices, body(): lax.all_gather(back, 'expert', axis=0, tiled=True)  82.7 us
    reduce_scatter x1, waiting for transfers between devices, body(): lax.psum_scatter((behind + jnp.dot(grad_up, up_mat.T, preferred_element_t...  80.5 us
    ppermute x2, waiting for transfers between devices, from_behind(): return lax.ppermute(x, axis, pairs)  39.6 us
    ppermute x2, starting transfers between devices, from_behind(): return lax.ppermute(x, axis, pairs)  10.2 us
    dot_general x1, matrix products, body(): jnp.dot(grad_up, up_mat.T, preferred_element_type=jnp.float32)  10.2 us
  transfers between devices with their start and end apart: 6, of which 6 were waited for; matrix products, arithmetic and copies ran while one was open for 4% of the time, Pallas kernels for 0%

commit v1 on v0

--- a/solution.py
+++ b/solution.py
@@ -56,7 +56,9 @@
         tiled=True,
     ).astype(jnp.float32)
     grad_hidden = jnp.dot(
-        lax.all_gather(back, "expert", axis=0, tiled=True),
+        jnp.concatenate(
+            lax.all_to_all(jnp.stack([back] * lax.axis_size("expert")), "expert", 0, 0), axis=0
+        ),
         down_mat.T,
         preferred_element_type=jnp.float32,
     )

time: 468 us -> 536 us (1.15)
  waiting for transfers between devices: 381 us -> 436 us
  starting transfers between devices: 10.6 us -> 21.1 us
    all_to_all x0 -> x1, waiting for transfers between devices: none -> 210 us  [body(): lax.all_to_all(jnp.stack([back] * lax.axis_size('expert')), 'expert', 0, 0)]
    all_gather x1 -> x0, waiting for transfers between devices: 82.7 us -> none  [body(): lax.all_gather(back, 'expert', axis=0, tiled=True)]
    all_gather x1, waiting for transfers between devices: 91.3 us -> 18.2 us  [body(): piece = lax.all_gather(sent, 'expert', axis=0, tiled=True)]
    all_to_all x0 -> x1, starting transfers between devices: none -> 10.1 us  [body(): lax.all_to_all(jnp.stack([back] * lax.axis_size('expert')), 'expert', 0, 0)]
  transfers between devices with their start and end apart: 6 -> 6, of which waited for: 6 -> 6; matrix products, arithmetic and copies ran while one was open for 4% -> 3% of each run, Pallas kernels for 0% -> 0%
where the time goes in v1:
time: 536 us
  waiting for transfers between devices  436 us (81%)
  matrix products  40.2 us (8%)
  starting transfers between devices  21.1 us (4%)
  local copies, waits for them, and re-layouts  15 us (3%)
  between operations  13.9 us (3%)
  other arithmetic  9.46 us (2%)
    all_to_all x1, waiting for transfers between devices, body(): lax.all_to_all(jnp.stack([back] * lax.axis_size('expert')), 'expert', 0, 0)  210 us
    reduce_scatter x1, waiting for transfers between devices, body(): lax.psum_scatter(jnp.dot(hidden, down_mat, preferred_element_type=jnp.flo...  87.4 us
    reduce_scatter x1, waiting for transfers between devices, body(): lax.psum_scatter((behind + jnp.dot(grad_up, up_mat.T, preferred_element_t...  80.8 us
    ppermute x2, waiting for transfers between devices, from_behind(): return lax.ppermute(x, axis, pairs)  39.7 us
    all_gather x1, waiting for transfers between devices, body(): piece = lax.all_gather(sent, 'expert', axis=0, tiled=True)  18.2 us
    ppermute x2, starting transfers between devices, from_behind(): return lax.ppermute(x, axis, pairs)  10.8 us
  transfers between devices with their start and end apart: 6, of which 6 were waited for; matrix products, arithmetic and copies ran while one was open for 3% of the time, Pallas kernels for 0%

profile of v1, /device:TPU:1, one launch (start us, length us, event | category | flops | bytes accessed | tf_op | source)
XLA Modules:
  0.0 535.7 jit_solution(5500474076872119954)
XLA Ops:
  7.2 0.0 copy-start
  7.2 0.9 select_reduce_fusion.1
  8.0 0.7 select_reduce_fusion
  8.8 2.0 convolution_convert_fusion.1
  10.8 3.8 stack.2
  14.6 10.1 %all-to-all-start = ((bf16[16,32,7168]{2,1,0:T(8,128)(2,1)}), bf16[16,32,7168]{2,1,0:T(8,128)(2,1)}, u32[]{:S(2)}, u32[]{:S(2)}) async-start(bf16[16,32,7168]{2,1,0:T(8,128)(2,1)} %stack.2), calls=%async_computation.1 | async-start | bytes 14680064 | tf_op jit(solution)/shard_map/all_to_all | solution.py:60
  24.7 0.0 all-gather.2.cloned.1.call-start
  24.7 2.6 convolution_convert_fusion.2
  27.4 0.0 all-gather.2.cloned.1.call-update
  27.4 0.0 reduce-scatter.5.cloned.1.call-start
  27.4 210.0 %all-to-all-done = bf16[16,32,7168]{2,1,0:T(8,128)(2,1)} async-done(((bf16[16,32,7168]{2,1,0:T(8,128)(2,1)}), bf16[16,32,7168]{2,1,0:T(8,128)(2,1)}, u32[]{:S(2)}, u32[]{:S(2)}) %all-to-all-start) | async-done | bytes 7340064 | tf_op jit(solution)/shard_map/all_to_all | solution.py:60
  237.4 5.7 %fusion.8 = f32[512,128]{1,0:T(8,128)S(1)} fusion(bf16[512,7168]{1,0:T(8,128)(2,1)} %bitcast.7, bf16[1,128,7168]{2,1,0:T(8,128)(2,1)} %param.17), kind=kOutput, calls=%fused_computation.17 | convolution fusion | flops 939524096 | bytes 9437184 | tf_op jit(solution)/shard_map/dot_general | solution.py:58
  243.1 18.2 %all-gather.2.cloned.1.call-done = bf16[512,7168]{1,0:T(8,128)(2,1)} async-done(((bf16[32,7168]{1,0:T(8,128)(2,1)}), bf16[512,7168]{1,0:T(8,128)(2,1)}) %all-gather.2.cloned.1.call-update) | async-done | bytes 7340048 | tf_op jit(solution)/shard_map/all_gather | solution.py:40
  261.3 0.0 copy-done
  261.3 0.0 copy-start.2
  261.3 0.0 copy-start.4
  261.3 5.3 fusion.16
  266.6 0.0 copy-done.2
  266.6 0.4 copy-done.4
  267.0 2.1 fusion.12
  269.1 7.3 %fusion.14 = f32[512,7168]{1,0:T(8,128)} fusion(bf16[1,7168,128]{2,1,0:T(8,128)(2,1)S(1)} %copy-done, f32[512,128]{1,0:T(8,128)S(1)} %fusion.16, f32[512,128]{1,0:T(8,128)S(1)} %fusion.8, f32[512,128]{1,0:T(8,128)S(1)} %fusion.12), kind=kOutput, calls=%fused_computation.23 | convolution fusion | flops 940179456 | bytes 17301504 | tf_op jit(solution)/shard_map/dot_general | solution.py:67
  276.4 10.2 %add_convert_fusion = bf16[512,7168]{1,0:T(8,128)(2,1)} fusion(f32[512,7168]{1,0:T(8,128)} %fusion.14, bf16[1,7168,128]{2,1,0:T(8,128)(2,1)S(1)} %copy-done.2, f32[512,128]{1,0:T(8,128)S(1)} %fusion.8, f32[512,128]{1,0:T(8,128)S(1)} %fusion.16), kind=kOutput, calls=%fused_computation.2 | convolution fusion | flops 947257344 | bytes 24379392 | tf_op jit(solution)/shard_map/dot_general | solution.py:69
  286.5 0.0 copy-start.3
  286.5 0.0 reduce-scatter.5.cloned.1.call-update
  286.6 0.2 reduce-scatter.3.cloned.1.call-start
  286.8 1.2 copy-done.3
  288.0 5.0 convolution_convert_fusion
  293.1 0.0 reduce-scatter.3.cloned.1.call-update
  293.1 80.8 %reduce-scatter.5.cloned.1.call-done = bf16[32,7168]{1,0:T(8,128)(2,1)} async-done(((bf16[512,7168]{1,0:T(8,128)(2,1)}), bf16[32,7168]{1,0:T(8,128)(2,1)}) %reduce-scatter.5.cloned.1.call-update) | async-done | bytes 458768 | tf_op jit(solution)/shard_map/reduce_scatter | solution.py:68
  374.0 1.1 convert_element_type.60
  375.1 3.6 gather_fusion.1
  378.6 87.4 %reduce-scatter.3.cloned.1.call-done = bf16[32,7168]{1,0:T(8,128)(2,1)} async-done(((bf16[512,7168]{1,0:T(8,128)(2,1)}), bf16[32,7168]{1,0:T(8,128)(2,1)}) %reduce-scatter.3.cloned.1.call-update) | async-done | bytes 458768 | tf_op jit(solution)/shard_map/reduce_scatter | solution.py:52
  466.0 1.1 convert_element_type.51
  467.1 3.4 gather_fusion
  470.5 5.7 %fusion.5 = (bf16[1,128,7168]{2,1,0:T(8,128)(2,1)S(1)}, bf16[1,128,7168]{2,1,0:T(8,128)(2,1)S(1)}) fusion(f32[128,7168]{1,0:T(8,128)} %gather_fusion.1, bf16[1,128,7168]{2,1,0:T(8,128)(2,1)} %param.11, pred[128]{0:T(512)(128)(4,1)S(1)} %compare_and_fusion, pred[128]{0:T(512)(128)(4,1)S(1)} %reduce_or.9, f32[128,7168]{1,0:T(8,128)} %gather_fusion, ...), kind=kLoop, calls=%fused_computation.15 | loop fusion | flops 9175040 | bytes 14680832 | tf_op jit(solution)/shard_map/broadcast_in_dim | solution.py:81
  476.2 8.7 %collective-permute-start = (bf16[1,128,7168]{2,1,0:T(8,128)(2,1)S(1)}, bf16[1,128,7168]{2,1,0:T(8,128)(2,1)S(1)}, u32[]{:S(2)}, u32[]{:S(2)}) collective-permute-start(bf16[1,128,7168]{2,1,0:T(8,128)(2,1)S(1)} %get-tuple-element.6), channel_id=1, source_target_pairs={{0,16},{16,32},{32,48},{48,64},{64,80},{80,96},{96,112},{112,128},... | collective-permute-start | bytes 5505032 | tf_op jit(solution)/shard_map/ppermute | solution.py:12
  484.9 0.0 copy-start.1
  485.0 2.1 collective-permute-start.1
  487.0 18.1 %collective-permute-done = bf16[1,128,7168]{2,1,0:T(8,128)(2,1)S(1)} collective-permute-done((bf16[1,128,7168]{2,1,0:T(8,128)(2,1)S(1)}, bf16[1,128,7168]{2,1,0:T(8,128)(2,1)S(1)}, u32[]{:S(2)}, u32[]{:S(2)}) %collective-permute-start) | collective-permute-done | bytes 1835040 | tf_op jit(solution)/shard_map/ppermute | solution.py:12
  505.1 21.6 %collective-permute-done.1 = bf16[1,128,7168]{2,1,0:T(8,128)(2,1)S(1)} collective-permute-done((bf16[1,128,7168]{2,1,0:T(8,128)(2,1)S(1)}, bf16[1,128,7168]{2,1,0:T(8,128)(2,1)S(1)}, u32[]{:S(2)}, u32[]{:S(2)}) %collective-permute-start.1) | collective-permute-done | bytes 1835040 | tf_op jit(solution)/shard_map/ppermute | solution.py:12
  526.7 1.2 copy.12
  527.9 1.2 copy.13
  529.2 0.0 copy-done.1
  (4 shorter events, 0.0 us)
Async XLA Ops:
  7.2 254.1 %copy-start = (bf16[1,7168,128]{2,1,0:T(8,128)(2,1)S(1)}, bf16[1,7168,128]{2,1,0:T(8,128)(2,1)}, u32[]{:S(2)}) copy-start(bf16[1,7168,128]{2,1,0:T(8,128)(2,1)} %param.15) | copy-start | bytes 5505028
  14.6 222.8 %all-to-all-start = ((bf16[16,32,7168]{2,1,0:T(8,128)(2,1)}), bf16[16,32,7168]{2,1,0:T(8,128)(2,1)}, u32[]{:S(2)}, u32[]{:S(2)}) async-start(bf16[16,32,7168]{2,1,0:T(8,128)(2,1)} %stack.2), calls=%async_computation.1 | async-start | bytes 14680064 | tf_op jit(solution)/shard_map/all_to_all | solution.py:60
  24.7 236.6 %all-gather.2.cloned.1.call-start = ((), (), s32[]{:S(2)}) async-start(), calls=%async_computation.3 | async-start | bytes 7798784 | tf_op jit(solution)/shard_map/all_gather | solution.py:40
  27.4 346.6 %reduce-scatter.5.cloned.1.call-start = ((), (), s32[]{:S(2)}) async-start(), calls=%async_computation.5 | async-start | bytes 7798784 | tf_op jit(solution)/shard_map/reduce_scatter | solution.py:68
  261.3 5.3 copy-start.2
  261.3 5.7 %copy-start.4 = (bf16[512,7168]{1,0:T(8,128)(2,1)S(1)}, bf16[512,7168]{1,0:T(8,128)(2,1)}, u32[]{:S(2)}) copy-start(bf16[512,7168]{1,0:T(8,128)(2,1)} %all-gather.2.cloned.1.call-done) | copy-start | bytes 22020100
  286.5 1.5 copy-start.3
  286.6 179.4 %reduce-scatter.3.cloned.1.call-start = ((), (), s32[]{:S(2)}) async-start(), calls=%async_computation.4 | async-start | bytes 7798784 | tf_op jit(solution)/shard_map/reduce_scatter | solution.py:52
  476.2 28.9 %collective-permute-start = (bf16[1,128,7168]{2,1,0:T(8,128)(2,1)S(1)}, bf16[1,128,7168]{2,1,0:T(8,128)(2,1)S(1)}, u32[]{:S(2)}, u32[]{:S(2)}) collective-permute-start(bf16[1,128,7168]{2,1,0:T(8,128)(2,1)S(1)} %get-tuple-element.6), channel_id=1, source_target_pairs={{0,16},{16,32},{32,48},{48,64},{64,80},{80,96},{96,112},{112,128},... | collective-permute-start | bytes 5505032 | tf_op jit(solution)/shard_map/ppermute | solution.py:12
  484.9 44.2 %copy-start.1 = (bf16[1,7168,128]{2,1,0:T(8,128)(2,1)S(1)}, bf16[1,7168,128]{2,1,0:T(8,128)(2,1)}, u32[]{:S(2)}) copy-start(bf16[1,7168,128]{2,1,0:T(8,128)(2,1)} %param.15) | copy-start | bytes 5505028
  485.0 41.7 %collective-permute-start.1 = (bf16[1,128,7168]{2,1,0:T(8,128)(2,1)S(1)}, bf16[1,128,7168]{2,1,0:T(8,128)(2,1)S(1)}, u32[]{:S(2)}, u32[]{:S(2)}) collective-permute-start(bf16[1,128,7168]{2,1,0:T(8,128)(2,1)S(1)} %get-tuple-element.5), channel_id=1, source_target_pairs={{16,0},{32,16},{48,32},{64,48},{80,64},{96,80},{112,96},{128,112},... | collective-permute-start | bytes 5505032 | tf_op jit(solution)/shard_map/ppermute | solution.py:12
Sparse Core Ops, SparseCore 0:
  27.8 233.3 all-gather.1
  286.7 87.2 reduce-scatter.4
  376.5 89.3 reduce-scatter.2
